TPU v7x, 128 devices: a whole 4x4x4 slice. The times are simulated.
128 devices in a mesh: req: 4 (over y), exp: 32 (over z, x, core).
Axes of the slice: x: 4, y: 4, z: 4, core: 2. Of those that a mesh axis runs over, the one named last changes fastest.
Arguments:
- states: bfloat16 [2, 16384, 1024], P(None, ('req', 'exp')), may hold values from -6 to 6
- lengths: int32 [128, 4], P(('req', 'exp')), may hold values from 1 to 64, 128 in all within a row
- targets: int32 [16384], P('req'), may hold values from 0 to 36863
- routes: int32 [2, 16384, 8], P(None, ('req', 'exp')), may hold values from 0 to 31, all different within a row; in each aligned block of 128 rows (0 to 127, 128 to 255, ..., all dimensions but the last counted through in order) at most 40 rows name the same one
- gate_probs: float32 [2, 16384, 8], P(None, ('req', 'exp')), may hold values from 0.02 to 0.4
- owners: int32 [512], P(('req', 'exp')), may hold values from 0 to 511, each once
- norm_gains: float32 [2, 3, 1024], replicated, may hold values from 0.25 to 1.75
- qkv_weight: bfloat16 [2, 1024, 2048], replicated, may hold values from -14 to 14
- out_weight: bfloat16 [2, 1024, 1024], replicated, may hold values from -0.1875 to 0.1875
- expert_in: bfloat16 [2, 32, 1024, 1024], P(None, 'exp'), may hold values from -0.1875 to 0.1875
- expert_down: bfloat16 [2, 32, 512, 1024], P(None, 'exp'), may hold values from -0.25 to 0.25
- vocab_head: bfloat16 [2, 36864, 1024], P(None, 'exp'), may hold values from -170 to 170
Outputs:
- token_logp: float32 [2, 16384], P(None, ('req', 'exp'))
- seq_totals: float32 [512], P(('req', 'exp'))
Inputs may be any that keep to these rules, and one draw needn't show every extreme that they name: `lengths`: each row sums to 128; some row reaches 64. `routes`: the 8 experts of a token are distinct; among the 128 tokens of one device, no expert is named by more than 40 of them for one model, and that bound is reached. `owners`: a permutation of the sequence numbers.
All inputs are finite; a program needn't handle non-finite values.
Results may differ from a plain program's by a relative error of at most 0.012.
The roundings to bfloat16 on the way count: a program that leaves them out, or rounds other values in their place, can miss the bound.
Values may be sent and summed in bfloat16 or wider, within the bound.
No kernel may reach another device: no remote copies, remote signals or barrier semaphores. Data moves between devices by JAX's collectives and lax.ppermute only.
A program may use at most 128 MiB of HBM per device.

v0:
```python
import jax
import jax.numpy as jnp
from jax import lax
from jax.sharding import PartitionSpec as P

HEADS = 16
KV_HEADS = 8
HEAD_DIM = 64
EXPERT_FF = 512
EXPERTS = 32
TOP = 8
CAP = 40
EPSILON = 1e-06
RESIDUAL_SCALE = 0.22
SCORE_SCALE = 0.015625
LOGIT_DIVISOR = 6.0
ROTARY_BASE = 10000.0


def combined_all(x, axis, combine):
    everything = jax.tree.map(lambda part: lax.all_gather(part, axis), x)
    initial = jax.tree.map(lambda part: part[0], everything)

    def step(k, so_far):
        return combine(so_far, jax.tree.map(lambda part: part[k], everything))

    return lax.fori_loop(1, lax.axis_size(axis), step, initial)


def root_norm(values, gain_row):
    values = values.astype(jnp.float32)
    scaled = lax.rsqrt(jnp.mean(values * values, axis=-1, keepdims=True) + EPSILON)
    return values * scaled * gain_row


def segment_table(length_row, token_count):
    seq_ends = jnp.cumsum(length_row)
    seq_starts = seq_ends - length_row
    places = jnp.arange(token_count, dtype=jnp.int32)
    segment = jnp.sum((places[:, None] >= seq_ends[None, :]).astype(jnp.int32), axis=1)
    member = segment[:, None] == jnp.arange(length_row.shape[0], dtype=jnp.int32)[None, :]
    position = places - jnp.sum(member.astype(jnp.int32) * seq_starts[None, :], axis=1)
    return (segment, member, position)


def rotary(values, position):
    half_dim = values.shape[-1] // 2
    frequency = ROTARY_BASE ** (-2.0 * jnp.arange(half_dim, dtype=jnp.float32) / values.shape[-1])
    angles = position.astype(jnp.float32)[:, None] * frequency[None, :]
    angles = jnp.concatenate([angles, angles], axis=-1)[:, None, :]
    leading = values[..., :half_dim]
    trailing = values[..., half_dim:]
    turned = jnp.concatenate([-trailing, leading], axis=-1)
    return values * jnp.cos(angles) + turned * jnp.sin(angles)


def attend(block_states, segment, position, gain_row, qkv_weight, out_weight):
    token_count = block_states.shape[0]
    group_size = HEADS // KV_HEADS
    normed = root_norm(block_states, gain_row).astype(jnp.bfloat16)
    mixed = jnp.dot(normed, qkv_weight, preferred_element_type=jnp.float32)
    queries = rotary(
        mixed[:, : HEADS * HEAD_DIM].reshape(token_count, HEADS, HEAD_DIM), position
    ).astype(jnp.bfloat16)
    keys_all = rotary(
        mixed[:, HEADS * HEAD_DIM : (HEADS + KV_HEADS) * HEAD_DIM].reshape(
            token_count, KV_HEADS, HEAD_DIM
        ),
        position,
    ).astype(jnp.bfloat16)
    values_all = (
        mixed[:, (HEADS + KV_HEADS) * HEAD_DIM :]
        .reshape(token_count, KV_HEADS, HEAD_DIM)
        .astype(jnp.bfloat16)
    )
    grouped = queries.reshape(token_count, KV_HEADS, group_size, HEAD_DIM)
    scores = (
        jnp.einsum("tgqd,sgd->gqts", grouped, keys_all, preferred_element_type=jnp.float32)
        * SCORE_SCALE
    )
    places = jnp.arange(token_count, dtype=jnp.int32)
    allowed = (segment[:, None] == segment[None, :]) & (places[None, :] <= places[:, None])
    scores = jnp.where(allowed, scores, -1e30)
    highest = jnp.max(scores, axis=-1, keepdims=True)
    weights = jnp.exp(scores - highest)
    weights = (weights / jnp.sum(weights, axis=-1, keepdims=True)).astype(jnp.bfloat16)
    attended = jnp.einsum(
        "gqts,sgd->tgqd", weights, values_all, preferred_element_type=jnp.float32
    ).astype(jnp.bfloat16)
    projected = jnp.dot(
        attended.reshape(token_count, HEADS * HEAD_DIM),
        out_weight,
        preferred_element_type=jnp.float32,
    )
    return (block_states.astype(jnp.float32) + RESIDUAL_SCALE * projected).astype(jnp.bfloat16)


def join_parts(first_part, second_part):
    first_max, first_mass, first_hit = first_part
    second_max, second_mass, second_hit = second_part
    joined_max = jnp.maximum(first_max, second_max)
    joined_mass = first_mass * jnp.exp(first_max - joined_max) + second_mass * jnp.exp(
        second_max - joined_max
    )
    return (joined_max, joined_mass, first_hit + second_hit)


def per_device(
    states,
    lengths,
    targets,
    routes,
    gate_probs,
    owners,
    norm_gains,
    qkv_weight,
    out_weight,
    expert_in,
    expert_down,
    vocab_head,
):
    token_count = states.shape[1]
    width = states.shape[2]
    segment, member, position = segment_table(lengths[0], token_count)
    residual = jnp.stack(
        [
            attend(
                states[which],
                segment,
                position,
                norm_gains[which, 0],
                qkv_weight[which],
                out_weight[which],
            )
            for which in range(2)
        ]
    )
    moe_in = root_norm(residual, norm_gains[:, 1][:, None, :]).astype(jnp.bfloat16)
    groups = lax.axis_size("exp")
    local_count = expert_in.shape[1]
    flat_routes = routes.reshape(2, token_count * TOP)
    onehot = (flat_routes[..., None] == jnp.arange(EXPERTS, dtype=jnp.int32)).astype(jnp.int32)
    rank_slot = jnp.sum((jnp.cumsum(onehot, axis=1) - 1) * onehot, axis=2)
    slot_index = (
        flat_routes * CAP + rank_slot + jnp.arange(2, dtype=jnp.int32)[:, None] * (EXPERTS * CAP)
    ).reshape(-1)
    token_index = jnp.arange(token_count * TOP, dtype=jnp.int32) // TOP
    outgoing = (
        jnp.zeros((2 * EXPERTS * CAP, width), jnp.bfloat16)
        .at[slot_index]
        .set(moe_in[:, token_index].reshape(-1, width))
    )
    arrived = lax.all_to_all(
        outgoing.reshape(2, groups, local_count * CAP, width),
        "exp",
        split_axis=1,
        concat_axis=1,
        tiled=True,
    )
    inputs = arrived.reshape(2, groups, local_count, CAP, width)
    gate_up = jnp.einsum("mslcd,mldf->mslcf", inputs, expert_in, preferred_element_type=jnp.float32)
    hidden = (jax.nn.silu(gate_up[..., :EXPERT_FF]) * gate_up[..., EXPERT_FF:]).astype(jnp.bfloat16)
    produced = jnp.einsum(
        "mslcf,mlfd->mslcd", hidden, expert_down, preferred_element_type=jnp.float32
    ).astype(jnp.bfloat16)
    returned = lax.all_to_all(
        produced.reshape(2, groups, local_count * CAP, width),
        "exp",
        split_axis=1,
        concat_axis=1,
        tiled=True,
    )
    picked = returned.reshape(2 * EXPERTS * CAP, width)[slot_index].reshape(
        2, token_count, TOP, width
    )
    mixture = jnp.sum(gate_probs[..., None] * picked.astype(jnp.float32), axis=2)
    final = root_norm(
        residual.astype(jnp.float32) + RESIDUAL_SCALE * mixture, norm_gains[:, 2][:, None, :]
    ).astype(jnp.bfloat16)
    shard = lax.axis_index("exp")
    vocab_rows = vocab_head.shape[1]
    lowest = shard * vocab_rows
    vocab_ids = jnp.arange(vocab_rows, dtype=jnp.int32)
    shard_piece = lax.all_gather(final, "exp", axis=1, tiled=True)
    piece_rows = shard_piece.shape[1]
    block_rows = 512
    block_count = piece_rows // block_rows
    wanted_all = targets - lowest

    def one_block(block_number):
        row_block = lax.dynamic_slice_in_dim(shard_piece, block_number * block_rows, block_rows, 1)
        wanted = lax.dynamic_slice_in_dim(wanted_all, block_number * block_rows, block_rows, 0)
        logits = (
            jnp.einsum("mtd,mvd->mtv", row_block, vocab_head, preferred_element_type=jnp.float32)
            / LOGIT_DIVISOR
        )
        highest = jnp.max(logits, axis=2)
        masses = jnp.sum(jnp.exp(logits - highest[..., None]), axis=2)
        chosen = jnp.sum(
            jnp.where(wanted[None, :, None] == vocab_ids[None, None, :], logits, 0.0), axis=2
        )
        return (highest, masses, chosen)

    block_max, block_mass, block_hit = lax.map(one_block, jnp.arange(block_count, dtype=jnp.int32))

    def place(fresh):
        ordered = jnp.transpose(fresh, (1, 0, 2)).reshape(2, piece_rows)
        return ordered

    part_max = place(block_max)
    part_mass = place(block_mass)
    part_hit = place(block_hit)
    all_max, all_mass, all_hit = combined_all((part_max, part_mass, part_hit), "exp", join_parts)
    begin = shard * token_count
    final_max = lax.dynamic_slice_in_dim(all_max, begin, token_count, 1)
    final_mass = lax.dynamic_slice_in_dim(all_mass, begin, token_count, 1)
    final_hit = lax.dynamic_slice_in_dim(all_hit, begin, token_count, 1)
    token_logp = final_hit - (final_max + jnp.log(final_mass))
    difference = token_logp[0] - token_logp[1]
    seq_sums = jnp.sum(member.astype(jnp.float32) * difference[:, None], axis=0)
    devices = lax.axis_size("req") * lax.axis_size("exp")
    everyone = devices * seq_sums.shape[0]
    dense_totals = jnp.sum(
        (owners[:, None] == jnp.arange(everyone, dtype=jnp.int32)[None, :]).astype(jnp.float32)
        * seq_sums[:, None],
        axis=0,
    )
    seq_totals = lax.psum_scatter(dense_totals, ("req", "exp"), scatter_dimension=0, tiled=True)
    return (token_logp, seq_totals)


def solution(mesh):
    in_specs = (
        P(None, ("req", "exp"), None),
        P(("req", "exp"), None),
        P("req"),
        P(None, ("req", "exp"), None),
        P(None, ("req", "exp"), None),
        P(("req", "exp")),
        P(),
        P(),
        P(),
        P(None, "exp", None, None),
        P(None, "exp", None, None),
        P(None, "exp", None),
    )
    out_specs = (P(None, ("req", "exp")), P(("req", "exp")))
    return jax.shard_map(
        per_device, mesh=mesh, in_specs=in_specs, out_specs=out_specs, check_vma=False
    )
```

profile of v0, /device:TPU:1, one launch (start us, length us, event | category | flops | bytes accessed | tf_op | source)
XLA Modules:
  0.0 671.6 jit_solution(7500306601122006520)
XLA Ops:
  47.5 15.8 %gather_fusion = bf16[1024,2,1024]{2,1,0:T(2,128)(2,1)} fusion(bf16[2,128,1024]{2,0,1:T(2,128)(2,1)S(1)} %copy.125, s32[1024]{0:T(1024)S(1)} %broadcast_clamp_fusion.1), kind=kCustom, calls=%fused_computation | custom fusion | bytes 8392704 | tf_op jit(solution)/shard_map/gather | solution.py:151
  68.9 18.0 %reduce-window.11 = s32[2,32,8,128]{3,2,1,0:T(8,128)S(1)} reduce-window(s32[2,32,8,128]{3,2,1,0:T(8,128)S(1)} %fusion.101, s32[]{:T(128)} %constant.119.clone.1), window={size=1x1x1x128 pad=0_0x0_0x0_0x127_0}, to_apply=%region_9.10 | reduce-window | flops 8323072 | bytes 524292 | tf_op jit(solution)/shard_map/reduce-window.1
  88.0 13.6 %scatter_custom_fusion = bf16[2560,1024]{1,0:T(8,128)(2,1)} fusion(s32[2048]{0:T(1024)S(1)} %bitcast.262, bf16[2048,1024]{1,0:T(8,128)(2,1)} %bitcast.240, bf16[]{:T(256)} %constant.129.clone.1), kind=kCustom, calls=%fused_computation.37 | custom fusion | bytes 5243392 | tf_op jit(solution)/shard_map/scatter | solution.py:151
  105.0 71.5 %all_to_all.10 = bf16[2,32,40,1024]{3,2,0,1:T(8,128)(2,1)S(1)} all-to-all(bf16[2,32,40,1024]{3,2,0,1:T(8,128)(2,1)S(1)} %copy.127), channel_id=1, replica_groups=mesh['req'=4,'exp'=32] {'exp'}, dimensions={1} | all-to-all | bytes 10485760 | tf_op jit(solution)/shard_map/all_to_all | solution.py:153
  176.5 8.2 %fusion.19 = f32[2,32,1,40,1024]{4,3,1,0,2:T(8,128)} fusion(bf16[2,1,1024,1024]{3,2,1,0:T(8,128)(2,1)S(1)} %copy-done.20, bf16[2,32,40,1024]{3,2,0,1:T(8,128)(2,1)S(1)} %all_to_all.10), kind=kOutput, calls=%fused_computation.34 | convolution fusion | flops 5368709120 | bytes 19922944 | tf_op jit(solution)/shard_map/mslcd,mldf->mslcf/dot_general | solution.py:161
  184.7 7.2 %convolution_convert_fusion = bf16[2,32,40,1024]{3,2,1,0:T(8,128)(2,1)S(1)} fusion(f32[2,32,1,40,1024]{4,3,1,0,2:T(8,128)} %fusion.19, bf16[2,1,512,1024]{3,2,1,0:T(8,128)(2,1)S(1)} %copy-done), kind=kOutput, calls=%fused_computation.35 | convolution fusion | flops 2694840320 | bytes 17825792 | tf_op jit(solution)/shard_map/mslcf,mlfd->mslcd/dot_general | solution.py:163
  200.2 61.7 %all-to-all-done.1 = bf16[2,32,40,1024]{3,2,0,1:T(8,128)(2,1)} async-done(((bf16[2,32,40,1024]{3,2,0,1:T(8,128)(2,1)}), bf16[2,32,40,1024]{3,2,0,1:T(8,128)(2,1)}, u32[]{:S(2)}, u32[]{:S(2)}) %all-to-all-start.1) | async-done | bytes 5242912 | tf_op jit(solution)/shard_map/all_to_all | solution.py:166
  261.9 5.6 copy.130
  267.5 14.1 %gather_fusion.1 = bf16[2048,1024]{1,0:T(8,128)(2,1)} fusion(bf16[2560,1024]{1,0:T(8,128)(2,1)} %bitcast.231, s32[2048]{0:T(1024)S(1)} %broadcast_clamp_fusion), kind=kCustom, calls=%fused_computation.1 | custom fusion | bytes 8396800 | tf_op jit(solution)/shard_map/gather | solution.py:173
  287.8 73.6 %all-gather.5.cloned.1.call-done = bf16[2,4096,1024]{2,1,0:T(8,128)(2,1)} async-done(((bf16[2,128,1024]{2,1,0:T(8,128)(2,1)}), bf16[2,4096,1024]{2,1,0:T(8,128)(2,1)}) %all-gather.5.cloned.1.call-update) | async-done | bytes 16777232 | tf_op jit(solution)/shard_map/all_gather | solution.py:184
  361.4 79.6 %while.35 = (s32[]{:T(128)}, f32[8,2,512]{2,1,0:T(2,128)S(1)}, f32[8,2,512]{2,1,0:T(2,128)}, f32[8,2,512]{2,1,0:T(2,128)}, s32[8]{0:T(128)S(1)}, /*index=5*/bf16...) while((s32[]{:T(128)}, f32[8,2,512]{2,1,0:T(2,128)S(1)}, ...), condition=%wide.region_20.21_spmd.clone, body=%wide.region_16.20_spmd.clone.sunk | while | flops 2423583744 | bytes 17480380 | solution.py:204
  362.7 6.0 fusion.161
  372.6 6.0 fusion.161
  382.6 6.0 fusion.161
  392.5 6.0 fusion.161
  402.5 6.0 fusion.161
  412.4 6.0 fusion.161
  422.4 6.0 fusion.161
  432.3 6.0 fusion.161
  442.4 40.9 %all-gather.11.cloned.1.call-done = f32[32,2,4096]{2,1,0:T(2,128)} async-done(((f32[1,2,4096]{2,1,0:T(2,128)}), f32[32,2,4096]{2,1,0:T(2,128)}) %all-gather.11.cloned.1.call-update) | async-done | bytes 1048592 | tf_op jit(solution)/shard_map/all_gather | solution.py:21
  484.0 43.5 %all-gather.9.cloned.1.call-done = f32[32,2,4096]{2,1,0:T(2,128)} async-done(((f32[1,2,4096]{2,1,0:T(2,128)}), f32[32,2,4096]{2,1,0:T(2,128)}) %all-gather.9.cloned.1.call-update) | async-done | bytes 1048592 | tf_op jit(solution)/shard_map/all_gather | solution.py:21
  528.2 43.4 %all-gather.7.cloned.1.call-done = f32[32,2,4096]{2,1,0:T(2,128)} async-done(((f32[1,2,4096]{2,1,0:T(2,128)}), f32[32,2,4096]{2,1,0:T(2,128)}) %all-gather.7.cloned.1.call-update) | async-done | bytes 1048592 | tf_op jit(solution)/shard_map/all_gather | solution.py:21
  572.4 27.7 %while.34 = (s32[]{:T(128)}, f32[2,4096]{1,0:T(2,128)S(1)}, f32[2,4096]{1,0:T(2,128)S(1)}, f32[2,4096]{1,0:T(2,128)S(1)}, f32[32,2,4096]{2,1,0:T(2,128)}, /*inde...) while((s32[]{:T(128)}, f32[2,4096]{1,0:T(2,128)S(1)}, ...), condition=%wide.region_22.23_spmd, body=%wide.region_21.22_spmd.sunk | while | flops 57349 | bytes 295059 | solution.py:27
  600.3 64.1 %all-reduce = f32[512]{0:T(512)S(1)} all-reduce(f32[512]{0:T(512)S(1)} %select_reduce_fusion.1), channel_id=2, replica_groups=mesh['req'=4,'exp'=32] {'req','exp'}, use_global_device_ids=true, to_apply=%region_25.26.clone | all-reduce | flops 512 | bytes 4096
  (219 shorter events, 122.4 us)
Async XLA Ops:
  7.2 177.5 %copy-start = (bf16[2,1,512,1024]{3,2,1,0:T(8,128)(2,1)S(1)}, bf16[2,1,512,1024]{3,2,1,0:T(8,128)(2,1)}, u32[]{:S(2)}) copy-start(bf16[2,1,512,1024]{3,2,1,0:T(8,128)(2,1)} %param.26) | copy-start | bytes 6291460
  9.3 5.2 copy-start.21
  12.4 1.0 copy-start.2
  25.7 6.6 copy-start.11
  25.7 7.2 %copy-start.8 = (s32[2,128,8]{1,2,0:T(8,128)S(1)}, s32[2,128,8]{1,2,0:T(8,128)}, u32[]{:S(2)}) copy-start(s32[2,128,8]{1,2,0:T(8,128)} %param.19) | copy-start | bytes 24580
  31.3 8.2 %copy-start.4 = (bf16[2,128,1024]{2,1,0:T(8,128)(2,1)S(1)}, bf16[2,128,1024]{2,1,0:T(8,128)(2,1)}, u32[]{:S(2)}) copy-start(bf16[2,128,1024]{2,1,0:T(8,128)(2,1)} %param.16) | copy-start | bytes 1572868
  39.4 5.0 copy-start.5
  41.6 5.9 copy-start.13
  63.3 5.6 copy-start.7
  63.3 24.2 %copy-start.6 = (s32[2,1024]{1,0:T(2,128)S(1)}, s32[2,1024]{1,0:T(2,128)}, u32[]{:S(2)}) copy-start(s32[2,1024]{1,0:T(2,128)} %eq.95) | copy-start | bytes 24580
  63.3 24.3 %copy-start.9 = (s32[2,128,8]{1,2,0:T(8,128)S(1)}, s32[2,128,8]{1,2,0:T(8,128)}, u32[]{:S(2)}) copy-start(s32[2,128,8]{1,2,0:T(8,128)} %broadcast_multiply_fusion.1) | copy-start | bytes 24580
  63.3 24.6 %copy-start.18 = (s32[2]{0:T(128)S(1)}, s32[2]{0:T(128)}, u32[]{:S(2)}) copy-start(s32[2]{0:T(128)} %iota_multiply_fusion) | copy-start | bytes 28
  105.0 71.5 %copy-start.20 = (bf16[2,1,1024,1024]{3,2,1,0:T(8,128)(2,1)S(1)}, bf16[2,1,1024,1024]{3,2,1,0:T(8,128)(2,1)}, u32[]{:S(2)}) copy-start(bf16[2,1,1024,1024]{3,2,1,0:T(8,128)(2,1)} %param.25) | copy-start | bytes 12582916
  195.0 5.0 copy-start.14
  195.0 66.9 %all-to-all-start.1 = ((bf16[2,32,40,1024]{3,2,0,1:T(8,128)(2,1)}), bf16[2,32,40,1024]{3,2,0,1:T(8,128)(2,1)}, u32[]{:S(2)}, u32[]{:S(2)}) async-start(bf16[2,32,40,1024]{3,2,0,1:T(8,128)(2,1)} %copy.129), calls=%async_computation.1 | async-start | bytes 10485760 | tf_op jit(solution)/shard_map/all_to_all | solution.py:166
  200.0 161.4 %all-gather.5.cloned.1.call-start = ((), (), s32[]{:S(2)}) async-start(), calls=%async_computation.2 | async-start | bytes 17301504 | tf_op jit(solution)/shard_map/all_gather | solution.py:184
  281.6 6.2 copy-start.12
  287.7 195.5 %all-gather.11.cloned.1.call-start = ((), (), s32[]{:S(2)}) async-start(), calls=%async_computation.5 | async-start | bytes 1081344 | tf_op jit(solution)/shard_map/all_gather | solution.py:21
  361.4 238.7 %copy-start.16 = (s32[128]{0:T(128)S(1)}, s32[128]{0:T(128)}, u32[]{:S(2)}) copy-start(s32[128]{0:T(128)} %copy-done.15) | copy-start | bytes 1540
  361.4 238.8 %copy-start.19 = (s32[4]{0:T(128)S(1)}, s32[4]{0:T(128)}, u32[]{:S(2)}) copy-start(s32[4]{0:T(128)} %param.21) | copy-start | bytes 52
  441.0 224.0 %copy-start.1 = (bf16[2,1,512,1024]{3,2,1,0:T(8,128)(2,1)S(1)}, bf16[2,1,512,1024]{3,2,1,0:T(8,128)(2,1)}, u32[]{:S(2)}) copy-start(bf16[2,1,512,1024]{3,2,1,0:T(8,128)(2,1)} %param.26) | copy-start | bytes 6291460
  441.0 86.4 %all-gather.9.cloned.1.call-start = ((), (), s32[]{:S(2)}) async-start(), calls=%async_computation.4 | async-start | bytes 1081344 | tf_op jit(solution)/shard_map/all_gather | solution.py:21
  441.8 129.8 %all-gather.7.cloned.1.call-start = ((), (), s32[]{:S(2)}) async-start(), calls=%async_computation.3 | async-start | bytes 1081344 | tf_op jit(solution)/shard_map/all_gather | solution.py:21
  600.1 65.0 %copy-start.17 = (f32[2,128]{1,0:T(2,128)}, f32[2,128]{1,0:T(2,128)S(1)}, u32[]{:S(2)}) copy-start(f32[2,128]{1,0:T(2,128)S(1)} %add_subtract_fusion) | copy-start | bytes 3076
  (3 other events, 2.4 us)
Sparse Core Ops, SparseCore 0:
  287.8 73.5 all-gather.4
  441.2 42.0 all-gather.10
  485.5 41.9 all-gather.8
  529.6 41.9 all-gather.6
where the time goes:
time: 675 us; the launch traced here: 672 us
  waiting for transfers between devices  264 us (39%)
  blocking collectives  136 us (20%)
  matrix products  88 us (13%)
  local copies, waits for them, and re-layouts  84.9 us (13%)
  other arithmetic  73.5 us (11%)
  between operations  14.3 us (2%)
    all_gather x3, waiting for transfers between devices, combined_all(): everything = jax.tree.map(lambda part: lax.all_gather(part, axis), x)  128 us
    all_gather x1, waiting for transfers between devices, per_device(): shard_piece = lax.all_gather(final, 'exp', axis=1, tiled=True)  73.6 us
    all_to_all x1, blocking collectives, per_device(): lax.all_to_all(outgoing.reshape(2, groups, local_count * CAP, width), 'ex...  71.5 us
    unnamed x1, blocking collectives  64.1 us
    all_to_all x1, waiting for transfers between devices, per_device(): lax.all_to_all(produced.reshape(2, groups, local_count * CAP, width), 'ex...  61.7 us
    dot_general x8, matrix products, one_block(): jnp.einsum('mtd,mvd->mtv', row_block, vocab_head, preferred_element_type=...  47.9 us
    add x31, other arithmetic, join_parts(): first_mass * jnp.exp(first_max - joined_max)  27.2 us
    gather x2, local copies, waits for them, and re-layouts, per_device(): moe_in[:, token_index].reshape(-1, width)  21.3 us
  transfers between devices with their start and end apart: 5, of which 5 were waited for; matrix products, arithmetic and copies ran while one was open for 0% of the time, Pallas kernels for 0%

commit v1 on v0

--- a/solution.py
+++ b/solution.py
@@ -181,7 +181,9 @@
     vocab_rows = vocab_head.shape[1]
     lowest = shard * vocab_rows
     vocab_ids = jnp.arange(vocab_rows, dtype=jnp.int32)
-    shard_piece = lax.all_gather(final, "exp", axis=1, tiled=True)
+    shard_piece = jnp.concatenate(
+        lax.all_to_all(jnp.stack([final] * lax.axis_size("exp")), "exp", 0, 0), axis=1
+    )
     piece_rows = shard_piece.shape[1]
     block_rows = 512
     block_count = piece_rows // block_rows

time: 675 us -> 840 us (1.24)
  waiting for transfers between devices: 264 us -> 401 us
  local copies, waits for them, and re-layouts: 84.9 us -> 105 us
  starting transfers between devices: 5.14 us -> 14.4 us
    all_to_all x0 -> x1, waiting for transfers between devices: none -> 201 us  [per_device(): lax.all_to_all(jnp.stack([final] * lax.axis_size('exp')), 'exp', 0, 0)]
    all_gather x1 -> x0, waiting for transfers between devices: 73.6 us -> none  [per_device(): shard_piece = lax.all_gather(final, 'exp', axis=1, tiled=True)]
    all_to_all x0 -> x1, local copies, waits for them, and re-layouts: none -> 13.9 us  [per_device(): lax.all_to_all(jnp.stack([final] * lax.axis_size('exp')), 'exp', 0, 0)]
    all_to_all x0 -> x1, starting transfers between devices: none -> 9.25 us  [per_device(): lax.all_to_all(jnp.stack([final] * lax.axis_size('exp')), 'exp', 0, 0)]
    all_gather x3, waiting for transfers between devices: 128 us -> 137 us  [combined_all(): everything = jax.tree.map(lambda part: lax.all_gather(part, axis), x)]
where the time goes in v1:
time: 840 us; the launch traced here: 837 us
  waiting for transfers between devices  401 us (48%)
  blocking collectives  136 us (16%)
  local copies, waits for them, and re-layouts  105 us (12%)
  matrix products  88.1 us (10%)
  other arithmetic  72.7 us (9%)
  starting transfers between devices  14.4 us (2%)
  between operations  14.3 us (2%)
    all_to_all x1, waiting for transfers between devices, per_device(): lax.all_to_all(jnp.stack([final] * lax.axis_size('exp')), 'exp', 0, 0)  201 us
    all_gather x3, waiting for transfers between devices, combined_all(): everything = jax.tree.map(lambda part: lax.all_gather(part, axis), x)  137 us
    all_to_all x1, blocking collectives, per_device(): lax.all_to_all(outgoing.reshape(2, groups, local_count * CAP, width), 'ex...  71.5 us
    unnamed x1, blocking collectives  64.1 us
    all_to_all x1, waiting for transfers between devices, per_device(): lax.all_to_all(produced.reshape(2, groups, local_count * CAP, width), 'ex...  61.8 us
    dot_general x8, matrix products, one_block(): jnp.einsum('mtd,mvd->mtv', row_block, vocab_head, preferred_element_type=...  47.9 us
    add x31, other arithmetic, join_parts(): first_mass * jnp.exp(first_max - joined_max)  27.2 us
    gather x2, local copies, waits for them, and re-layouts, per_device(): moe_in[:, token_index].reshape(-1, width)  21.3 us
  transfers between devices with their start and end apart: 5, of which 5 were waited for; matrix products, arithmetic and copies ran while one was open for 0% of the time, Pallas kernels for 0%

profile of v1, /device:TPU:1, one launch (start us, length us, event | category | flops | bytes accessed | tf_op | source)
XLA Modules:
  0.0 836.9 jit_solution(8522667930521256179)
XLA Ops:
  47.5 15.8 %gather_fusion = bf16[1024,2,1024]{2,1,0:T(2,128)(2,1)} fusion(bf16[2,128,1024]{2,0,1:T(2,128)(2,1)S(1)} %copy.126, s32[1024]{0:T(1024)S(1)} %broadcast_clamp_fusion.1), kind=kCustom, calls=%fused_computation | custom fusion | bytes 8392704 | tf_op jit(solution)/shard_map/gather | solution.py:151
  68.8 18.0 %reduce-window.11 = s32[2,32,8,128]{3,2,1,0:T(8,128)S(1)} reduce-window(s32[2,32,8,128]{3,2,1,0:T(8,128)S(1)} %fusion.101, s32[]{:T(128)} %constant.119.clone.1), window={size=1x1x1x128 pad=0_0x0_0x0_0x127_0}, to_apply=%region_9.10 | reduce-window | flops 8323072 | bytes 524292 | tf_op jit(solution)/shard_map/reduce-window.1
  88.0 13.6 %scatter_custom_fusion = bf16[2560,1024]{1,0:T(8,128)(2,1)} fusion(s32[2048]{0:T(1024)S(1)} %bitcast.266, bf16[2048,1024]{1,0:T(8,128)(2,1)} %bitcast.244, bf16[]{:T(256)} %constant.129.clone.1), kind=kCustom, calls=%fused_computation.37 | custom fusion | bytes 5243392 | tf_op jit(solution)/shard_map/scatter | solution.py:151
  104.9 71.5 %all_to_all.15 = bf16[2,32,40,1024]{3,2,0,1:T(8,128)(2,1)S(1)} all-to-all(bf16[2,32,40,1024]{3,2,0,1:T(8,128)(2,1)S(1)} %copy.128), channel_id=1, replica_groups=mesh['req'=4,'exp'=32] {'exp'}, dimensions={1} | all-to-all | bytes 10485760 | tf_op jit(solution)/shard_map/all_to_all | solution.py:153
  176.4 8.2 fusion.19
  184.6 7.2 convolution_convert_fusion
  200.1 61.8 %all-to-all-done.1 = bf16[2,32,40,1024]{3,2,0,1:T(8,128)(2,1)} async-done(((bf16[2,32,40,1024]{3,2,0,1:T(8,128)(2,1)}), bf16[2,32,40,1024]{3,2,0,1:T(8,128)(2,1)}, u32[]{:S(2)}, u32[]{:S(2)}) %all-to-all-start.1) | async-done | bytes 5242912 | tf_op jit(solution)/shard_map/all_to_all | solution.py:166
  267.4 14.1 %gather_fusion.1 = bf16[2048,1024]{1,0:T(8,128)(2,1)} fusion(bf16[2560,1024]{1,0:T(8,128)(2,1)} %bitcast.234, s32[2048]{0:T(1024)S(1)} %broadcast_clamp_fusion), kind=kCustom, calls=%fused_computation.1 | custom fusion | bytes 8396800 | tf_op jit(solution)/shard_map/gather | solution.py:173
  286.8 6.0 stack.11
  292.8 9.3 %all-to-all-start.2 = ((bf16[32,2,128,1024]{3,2,1,0:T(8,128)(2,1)}), bf16[32,2,128,1024]{3,2,1,0:T(8,128)(2,1)}, u32[]{:S(2)}, u32[]{:S(2)}) async-start(bf16[32,2,128,1024]{3,2,1,0:T(8,128)(2,1)} %stack.11), calls=%async_computation.2 | async-start | bytes 33554432 | tf_op jit(solution)/shard_map/all_to_all | solution.py:185
  302.2 201.5 %all-to-all-done.2 = bf16[32,2,128,1024]{3,2,1,0:T(8,128)(2,1)} async-done(((bf16[32,2,128,1024]{3,2,1,0:T(8,128)(2,1)}), bf16[32,2,128,1024]{3,2,1,0:T(8,128)(2,1)}, u32[]{:S(2)}, u32[]{:S(2)}) %all-to-all-start.2) | async-done | bytes 16777248 | tf_op jit(solution)/shard_map/all_to_all | solution.py:185
  503.7 13.9 %copy.132 = bf16[32,2,128,1024]{3,2,0,1:T(8,128)(2,1)} copy(bf16[32,2,128,1024]{3,2,1,0:T(8,128)(2,1)} %all-to-all-done.2) | data formatting | bytes 33554432 | tf_op jit(solution)/shard_map/all_to_all | solution.py:185
  517.6 79.6 %while.35 = (s32[]{:T(128)}, f32[8,2,512]{2,1,0:T(2,128)S(1)}, f32[8,2,512]{2,1,0:T(2,128)}, f32[8,2,512]{2,1,0:T(2,128)}, s32[8]{0:T(128)S(1)}, /*index=5*/bf16...) while((s32[]{:T(128)}, f32[8,2,512]{2,1,0:T(2,128)S(1)}, ...), condition=%wide.region_20.21_spmd.clone, body=%wide.region_16.20_spmd.clone.sunk | while | flops 2423583744 | bytes 17480380 | solution.py:206
  518.8 6.0 fusion.161
  528.8 6.0 fusion.161
  538.7 6.0 fusion.161
  548.7 6.0 fusion.161
  568.5 6.0 fusion.161
  588.4 6.0 fusion.161
  598.7 49.8 %all-gather.8.cloned.1.call-done = f32[32,2,4096]{2,1,0:T(2,128)} async-done(((f32[1,2,4096]{2,1,0:T(2,128)}), f32[32,2,4096]{2,1,0:T(2,128)}) %all-gather.8.cloned.1.call-update) | async-done | bytes 1048592 | tf_op jit(solution)/shard_map/all_gather | solution.py:21
  649.2 43.5 %all-gather.6.cloned.1.call-done = f32[32,2,4096]{2,1,0:T(2,128)} async-done(((f32[1,2,4096]{2,1,0:T(2,128)}), f32[32,2,4096]{2,1,0:T(2,128)}) %all-gather.6.cloned.1.call-update) | async-done | bytes 1048592 | tf_op jit(solution)/shard_map/all_gather | solution.py:21
  693.4 43.5 %all-gather.4.cloned.1.call-done = f32[32,2,4096]{2,1,0:T(2,128)} async-done(((f32[1,2,4096]{2,1,0:T(2,128)}), f32[32,2,4096]{2,1,0:T(2,128)}) %all-gather.4.cloned.1.call-update) | async-done | bytes 1048592 | tf_op jit(solution)/shard_map/all_gather | solution.py:21
  737.7 27.7 %while.34 = (s32[]{:T(128)}, f32[2,4096]{1,0:T(2,128)S(1)}, f32[2,4096]{1,0:T(2,128)S(1)}, f32[2,4096]{1,0:T(2,128)S(1)}, f32[32,2,4096]{2,1,0:T(2,128)}, /*inde...) while((s32[]{:T(128)}, f32[2,4096]{1,0:T(2,128)S(1)}, ...), condition=%wide.region_22.23_spmd, body=%wide.region_21.22_spmd.sunk | while | flops 57349 | bytes 295059 | solution.py:27
  765.6 64.1 %all-reduce = f32[512]{0:T(512)S(1)} all-reduce(f32[512]{0:T(512)S(1)} %select_reduce_fusion.1), channel_id=2, replica_groups=mesh['req'=4,'exp'=32] {'req','exp'}, use_global_device_ids=true, to_apply=%region_25.26.clone | all-reduce | flops 512 | bytes 4096
  (220 shorter events, 139.2 us)
Async XLA Ops:
  7.2 177.4 %copy-start = (bf16[2,1,512,1024]{3,2,1,0:T(8,128)(2,1)S(1)}, bf16[2,1,512,1024]{3,2,1,0:T(8,128)(2,1)}, u32[]{:S(2)}) copy-start(bf16[2,1,512,1024]{3,2,1,0:T(8,128)(2,1)} %param.26) | copy-start | bytes 6291460
  9.3 5.2 copy-start.21
  12.4 1.0 copy-start.2
  25.6 6.6 copy-start.11
  25.6 7.2 copy-start.8
  31.2 8.2 copy-start.4
  39.4 5.0 copy-start.5
  41.6 5.9 copy-start.13
  63.2 5.6 copy-start.7
  63.3 24.2 %copy-start.6 = (s32[2,1024]{1,0:T(2,128)S(1)}, s32[2,1024]{1,0:T(2,128)}, u32[]{:S(2)}) copy-start(s32[2,1024]{1,0:T(2,128)} %eq.95) | copy-start | bytes 24580
  63.3 24.3 %copy-start.9 = (s32[2,128,8]{1,2,0:T(8,128)S(1)}, s32[2,128,8]{1,2,0:T(8,128)}, u32[]{:S(2)}) copy-start(s32[2,128,8]{1,2,0:T(8,128)} %broadcast_multiply_fusion.1) | copy-start | bytes 24580
  63.3 24.6 %copy-start.18 = (s32[2]{0:T(128)S(1)}, s32[2]{0:T(128)}, u32[]{:S(2)}) copy-start(s32[2]{0:T(128)} %iota_multiply_fusion) | copy-start | bytes 28
  104.9 71.5 %copy-start.20 = (bf16[2,1,1024,1024]{3,2,1,0:T(8,128)(2,1)S(1)}, bf16[2,1,1024,1024]{3,2,1,0:T(8,128)(2,1)}, u32[]{:S(2)}) copy-start(bf16[2,1,1024,1024]{3,2,1,0:T(8,128)(2,1)} %param.25) | copy-start | bytes 12582916
  195.0 5.0 copy-start.14
  195.0 66.9 %all-to-all-start.1 = ((bf16[2,32,40,1024]{3,2,0,1:T(8,128)(2,1)}), bf16[2,32,40,1024]{3,2,0,1:T(8,128)(2,1)}, u32[]{:S(2)}, u32[]{:S(2)}) async-start(bf16[2,32,40,1024]{3,2,0,1:T(8,128)(2,1)} %copy.130), calls=%async_computation.1 | async-start | bytes 10485760 | tf_op jit(solution)/shard_map/all_to_all | solution.py:166
  292.8 9.4 %copy-start.12 = (s32[4096]{0:T(1024)S(1)}, s32[4096]{0:T(1024)}, u32[]{:S(2)}) copy-start(s32[4096]{0:T(1024)} %param.18) | copy-start | bytes 49156
  292.8 210.8 %all-to-all-start.2 = ((bf16[32,2,128,1024]{3,2,1,0:T(8,128)(2,1)}), bf16[32,2,128,1024]{3,2,1,0:T(8,128)(2,1)}, u32[]{:S(2)}, u32[]{:S(2)}) async-start(bf16[32,2,128,1024]{3,2,1,0:T(8,128)(2,1)} %stack.11), calls=%async_computation.2 | async-start | bytes 33554432 | tf_op jit(solution)/shard_map/all_to_all | solution.py:185
  302.1 346.3 %all-gather.8.cloned.1.call-start = ((), (), s32[]{:S(2)}) async-start(), calls=%async_computation.5 | async-start | bytes 1081344 | tf_op jit(solution)/shard_map/all_gather | solution.py:21
  517.6 247.9 %copy-start.16 = (s32[128]{0:T(128)S(1)}, s32[128]{0:T(128)}, u32[]{:S(2)}) copy-start(s32[128]{0:T(128)} %copy-done.15) | copy-start | bytes 1540
  517.6 248.0 %copy-start.19 = (s32[4]{0:T(128)S(1)}, s32[4]{0:T(128)}, u32[]{:S(2)}) copy-start(s32[4]{0:T(128)} %param.21) | copy-start | bytes 52
  597.1 233.2 %copy-start.1 = (bf16[2,1,512,1024]{3,2,1,0:T(8,128)(2,1)S(1)}, bf16[2,1,512,1024]{3,2,1,0:T(8,128)(2,1)}, u32[]{:S(2)}) copy-start(bf16[2,1,512,1024]{3,2,1,0:T(8,128)(2,1)} %param.26) | copy-start | bytes 6291460
  597.2 95.5 %all-gather.6.cloned.1.call-start = ((), (), s32[]{:S(2)}) async-start(), calls=%async_computation.4 | async-start | bytes 1081344 | tf_op jit(solution)/shard_map/all_gather | solution.py:21
  597.9 139.0 %all-gather.4.cloned.1.call-start = ((), (), s32[]{:S(2)}) async-start(), calls=%async_computation.3 | async-start | bytes 1081344 | tf_op jit(solution)/shard_map/all_gather | solution.py:21
  765.4 65.0 %copy-start.17 = (f32[2,128]{1,0:T(2,128)}, f32[2,128]{1,0:T(2,128)S(1)}, u32[]{:S(2)}) copy-start(f32[2,128]{1,0:T(2,128)S(1)} %add_subtract_fusion) | copy-start | bytes 3076
  (3 other events, 2.3 us)
Sparse Core Ops, SparseCore 0:
  597.3 51.0 all-gather.7
  650.7 41.9 all-gather.5
  694.9 41.9 all-gather.3
